TPU v7x, 32 devices: a whole 2x2x4 slice. The times are simulated.
32 devices in a mesh: replica: 8 (over z, x), tensor: 4 (over y, core).
Axes of the slice: x: 2, y: 2, z: 4, core: 2. Of those that a mesh axis runs over, the one named last changes fastest.
Arguments:
- hidden: bfloat16 [256, 8192], P('replica', 'tensor'), may hold values from -600 to 600
- input_norm_gain: float32 [8192], replicated, may hold values from 0.1 to 1.9
- key_value_weight: bfloat16 [8192, 2, 1024], P(None, None, 'tensor'), may hold values from -0.0625 to 0.0625
- adapter_down: bfloat16 [128, 8192, 128], P('replica', 'tensor'), may hold values from -0.0625 to 0.0625
- adapter_up: bfloat16 [128, 2, 64, 1024], P('replica', None, None, 'tensor'), may hold values from -0.75 to 0.75
- query: bfloat16 [256, 8192], P('replica', 'tensor'), may hold values from -6 to 6
- key_value_cache: bfloat16 [256, 512, 2, 1024], P('replica', None, None, 'tensor'), may hold values from -6 to 6
- segment_adapter: int32 [8, 16], P('replica'), may hold values from 0 to 127, as said below
- segment_sizes: int32 [8, 16], P('replica'), may hold values from 1 to 4, 32 in all within a row
- cached_length: int32 [256], P('replica'), may hold values from 2 to 512, as said below
Outputs:
- new_kv: bfloat16 [256, 2, 1024], P('replica', None, 'tensor')
- attended: bfloat16 [256, 8192], P('replica', 'tensor')
Inputs may be any that keep to these rules, and one draw needn't show every extreme that they name: `segment_adapter`: the segments of one replica name distinct adapters; adapter a is stored at index a // 16 of replica. At most 2 of one replica's segments name adapters stored at one index of replica, and in every replica's list some index of replica is named exactly 2 times. `segment_sizes`: the sizes of one replica's segments sum to 32. The new token takes position cached_length.
All inputs are finite; a program needn't handle non-finite values.
Results may differ from a plain program's by a relative error of at most 0.0058.
Values may be sent and summed in bfloat16 or wider, within the bound.
No kernel may reach another device: no remote copies, remote signals or barrier semaphores. Data moves between devices by JAX's collectives and lax.ppermute only.
A program may use at most 192 MiB of HBM per device.

v0:
```python
import jax
import jax.numpy as jnp
from jax import lax
from jax.sharding import PartitionSpec as P

HEAD = 128
ADP_DEV = 16
SLOT = 4
CAP = 2
ADAPTER_SCALE = 0.5
ROPE_BASE = 500000.0
EPSILON = 1e-05


def rotate(key_heads, token_position):
    half_size = key_heads.shape[-1] // 2
    inv_freq = ROPE_BASE ** (
        -(jnp.arange(half_size, dtype=jnp.float32) * 2.0) / key_heads.shape[-1]
    )
    angles = token_position.astype(jnp.float32)[:, None] * inv_freq[None, :]
    cosine_term = jnp.cos(angles)[:, None, :]
    sine_term = jnp.sin(angles)[:, None, :]
    first_half = key_heads[..., :half_size]
    second_half = key_heads[..., half_size:]
    return jnp.concatenate(
        [
            first_half * cosine_term - second_half * sine_term,
            second_half * cosine_term + first_half * sine_term,
        ],
        axis=-1,
    )


def body(
    hidden,
    input_norm_gain,
    key_value_weight,
    adapter_down,
    adapter_up,
    query,
    key_value_cache,
    segment_adapter,
    segment_sizes,
    cached_length,
):
    row_count = hidden.shape[0]
    part_width = hidden.shape[1]
    kv_width = key_value_weight.shape[2]
    kv_local = kv_width // HEAD
    cache_len = key_value_cache.shape[1]
    adapter_rank_size = adapter_up.shape[2]
    replicas = lax.axis_size("replica")
    segments = segment_sizes.shape[1]
    gathered = lax.all_gather(hidden, "tensor", axis=1, tiled=True)
    widened = gathered.astype(jnp.float32)
    normed = (
        widened
        * lax.rsqrt(jnp.mean(widened * widened, axis=1, keepdims=True) + EPSILON)
        * input_norm_gain
    ).astype(jnp.bfloat16)
    own_cols = lax.dynamic_slice_in_dim(
        normed, lax.axis_index("tensor") * part_width, part_width, 1
    )
    seg_counts = segment_sizes[0]
    adapters = segment_adapter[0]
    seg_ends = jnp.cumsum(seg_counts, dtype=jnp.int32)
    starts = seg_ends - seg_counts
    offsets = jnp.arange(SLOT, dtype=jnp.int32)
    row_ids = jnp.arange(row_count, dtype=jnp.int32)
    segment_index = jnp.sum((seg_ends[None, :] <= row_ids[:, None]).astype(jnp.int32), axis=1)
    token_position = row_ids - starts[segment_index]
    owners = adapters // ADP_DEV
    local_ids = adapters % ADP_DEV
    seg_ids = jnp.arange(segments, dtype=jnp.int32)
    slot_rank = jnp.sum(
        ((owners[None, :] == owners[:, None]) & (seg_ids[None, :] < seg_ids[:, None])).astype(
            jnp.int32
        ),
        axis=1,
    )
    owner_hit = (owners[None, None, :] == jnp.arange(replicas, dtype=jnp.int32)[:, None, None]) & (
        slot_rank[None, None, :] == jnp.arange(CAP, dtype=jnp.int32)[None, :, None]
    )
    wanted = jnp.sum(jnp.where(owner_hit, local_ids[None, None, :], 0), axis=2)
    fetch_slot = owners * CAP + slot_rank
    seg_at = jnp.sum(jnp.where(owner_hit, seg_ids[None, None, :], 0), axis=2)
    filled = jnp.any(owner_hit, axis=2)
    slot_counts = jnp.where(filled, seg_counts[seg_at], 0)
    slot_live = offsets[None, None, :] < slot_counts[:, :, None]
    source_row = jnp.where(slot_live, starts[seg_at][:, :, None] + offsets[None, None, :], 0)
    slot_rows = jnp.where(
        slot_live[:, :, :, None], own_cols[source_row], jnp.zeros((), jnp.bfloat16)
    )
    segment_member_mask = lax.all_to_all(wanted, "replica", split_axis=0, concat_axis=0, tiled=True)
    selected_down = adapter_down[segment_member_mask]
    selected_up = adapter_up[segment_member_mask]
    down_got = lax.all_to_all(selected_down, "replica", split_axis=0, concat_axis=0, tiled=True)
    up_got = lax.all_to_all(selected_up, "replica", split_axis=0, concat_axis=0, tiled=True)
    partial_value = jnp.einsum(
        "oksd,okdr->oksr", slot_rows, down_got, preferred_element_type=jnp.float32
    )
    summed = lax.psum(partial_value, "tensor").astype(jnp.bfloat16)
    summed = summed.reshape(summed.shape[:3] + (2, adapter_rank_size))
    slot_delta = (
        jnp.einsum("okscr,okcrw->okscw", summed, up_got, preferred_element_type=jnp.float32)
        * ADAPTER_SCALE
    )
    flat_delta = slot_delta.reshape((replicas * CAP * SLOT,) + slot_delta.shape[3:])
    adapter_delta = flat_delta[fetch_slot[segment_index] * SLOT + token_position]
    base_projection = jnp.dot(
        normed,
        key_value_weight.reshape(key_value_weight.shape[0], 2 * kv_width),
        preferred_element_type=jnp.float32,
    ).reshape(row_count, 2, kv_width)
    current_key_value = base_projection + adapter_delta
    rotated = rotate(
        current_key_value[:, 0].reshape(row_count, kv_local, HEAD), cached_length
    ).reshape(row_count, kv_width)
    new_kv = jnp.stack([rotated, current_key_value[:, 1]], axis=1).astype(jnp.bfloat16)
    group_size = query.shape[1] // HEAD // kv_local
    scale = float(HEAD) ** (-0.5)
    query_heads = query.reshape(row_count, kv_local, group_size, HEAD)
    cached_keys = key_value_cache[:, :, 0].reshape(row_count, cache_len, kv_local, HEAD)
    cached_values = key_value_cache[:, :, 1].reshape(row_count, cache_len, kv_local, HEAD)
    scores = (
        jnp.einsum("bhgd,bthd->bhgt", query_heads, cached_keys, preferred_element_type=jnp.float32)
        * scale
    )
    is_live = jnp.arange(cache_len, dtype=jnp.int32)[None, :] < cached_length[:, None]
    scores = jnp.where(is_live[:, None, None, :], scores, -jnp.inf)
    new_key = new_kv[:, 0].reshape(row_count, kv_local, HEAD)
    new_value = new_kv[:, 1].astype(jnp.float32).reshape(row_count, kv_local, HEAD)
    own_score = (
        jnp.einsum("bhgd,bhd->bhg", query_heads, new_key, preferred_element_type=jnp.float32)
        * scale
    )
    top_score = jnp.maximum(jnp.max(scores, axis=-1), own_score)
    weights = jnp.exp(scores - top_score[..., None])
    own_weight = jnp.exp(own_score - top_score)
    total_mass = jnp.sum(weights, axis=-1) + own_weight
    prob_rows = (weights / total_mass[..., None]).astype(jnp.bfloat16)
    own_prob = (own_weight / total_mass).astype(jnp.bfloat16)
    context = jnp.einsum(
        "bhgt,bthd->bhgd", prob_rows, cached_values, preferred_element_type=jnp.float32
    )
    context = context + own_prob.astype(jnp.float32)[..., None] * new_value[:, :, None, :]
    attended = context.reshape(row_count, kv_local * group_size * HEAD).astype(jnp.bfloat16)
    return (new_kv, attended)


def solution(mesh):
    in_specs = (
        P("replica", "tensor"),
        P(),
        P(None, None, "tensor"),
        P("replica", "tensor", None),
        P("replica", None, None, "tensor"),
        P("replica", "tensor"),
        P("replica", None, None, "tensor"),
        P("replica", None),
        P("replica", None),
        P("replica"),
    )
    out_specs = (P("replica", None, "tensor"), P("replica", "tensor"))
    return jax.shard_map(body, mesh=mesh, in_specs=in_specs, out_specs=out_specs, check_vma=False)
```

profile of v0, /device:TPU:0, one launch (start us, length us, event | category | flops | bytes accessed | tf_op | source)
XLA Modules:
  0.0 256.9 jit_solution(18434199444916356622)
XLA Ops:
  0.6 0.8 fusion.26
  1.4 0.7 and_select_fusion.2
  2.5 13.5 %all_to_all.22 = s32[8,1,2]{2,1,0:T(1,128)S(1)} all-to-all(s32[8,1,2]{2,1,0:T(1,128)S(1)} %copy.82), channel_id=1, replica_groups=mesh['replica'=8,'tensor'=4] {'replica'}, dimensions={0} | all-to-all | bytes 128 | tf_op jit(solution)/shard_map/all_to_all | solution.py:94
  16.3 8.1 %gather_fusion.4 = bf16[16,2048,128]{2,1,0:T(8,128)(2,1)} fusion(bf16[16,2048,128]{2,1,0:T(8,128)(2,1)} %param.13, s32[1024]{0:T(1024)S(1)} %pad_clamp_fusion.4), kind=kCustom, calls=%fused_computation.4 | custom fusion | bytes 16777280 | tf_op jit(solution)/shard_map/gather | solution.py:95
  24.4 5.0 %all-to-all-start.2 = ((bf16[8,2,2048,128]{3,2,1,0:T(8,128)(2,1)}), bf16[8,2,2048,128]{3,2,1,0:T(8,128)(2,1)}, u32[]{:S(2)}, u32[]{:S(2)}) async-start(bf16[8,2,2048,128]{3,2,1,0:T(8,128)(2,1)} %bitcast.100), calls=%async_computation.2 | async-start | bytes 16777216 | tf_op jit(solution)/shard_map/all_to_all | solution.py:97
  29.4 8.0 %copy.109 = bf16[1024,8,2,256]{3,1,2,0:T(8,128)(2,1)} copy(bf16[1024,8,2,256]{3,2,1,0:T(2,128)(2,1)} %bitcast.104) | data formatting | bytes 16777216
  37.4 11.3 %copy.81 = bf16[512,8192]{1,0:T(8,128)(2,1)} copy(bf16[512,8192]{0,1:T(8,128)(2,1)} %bitcast.102) | data formatting | bytes 16777216 | tf_op jit(solution)/shard_map/dot_general | solution.py:110
  49.2 0.7 gather_fusion.2
  49.9 0.7 gather_fusion.1
  51.2 7.2 %all_gather.3 = bf16[32,8192]{1,0:T(8,128)(2,1)S(1)} all-gather(bf16[32,2048]{1,0:T(8,128)(2,1)S(1)} %copy-done.3), channel_id=1, replica_groups=mesh['replica'=8,'tensor'=4] {'tensor'}, dimensions={1}, use_global_device_ids=true | all-gather | bytes 655360 | tf_op jit(solution)/shard_map/all_gather | solution.py:54
  58.9 0.8 copy-done.2
  59.7 0.7 gather_fusion.3
  60.6 1.3 gather_fusion.6
  61.9 1.3 gather_fusion.5
  63.7 33.0 %fusion.28 = (bf16[32,512,1,256]{3,2,1,0:T(2,128)(2,1)}, bf16[32,512,1,256]{3,2,1,0:T(2,128)(2,1)}) fusion(bf16[32,512,2,256]{3,2,1,0:T(2,128)(2,1)} %param.16), kind=kLoop, calls=%fused_computation.94 | loop fusion | bytes 33554432 | tf_op jit(solution)/shard_map/slice | solution.py:123
  96.7 35.5 %copy.108 = bf16[32,512,1,256]{1,3,0,2:T(8,128)(2,1)} copy(bf16[32,512,1,256]{3,2,1,0:T(2,128)(2,1)} %get-tuple-element.17) | data formatting | bytes 16777216
  132.2 35.6 %copy.107 = bf16[32,512,1,256]{1,3,0,2:T(8,128)(2,1)} copy(bf16[32,512,1,256]{3,2,1,0:T(2,128)(2,1)} %get-tuple-element.16) | data formatting | bytes 16777216
  167.9 1.7 gather_fusion
  169.6 41.7 %all-to-all-done.2 = bf16[8,2,2048,128]{3,2,1,0:T(8,128)(2,1)} async-done(((bf16[8,2,2048,128]{3,2,1,0:T(8,128)(2,1)}), bf16[8,2,2048,128]{3,2,1,0:T(8,128)(2,1)}, u32[]{:S(2)}, u32[]{:S(2)}) %all-to-all-start.2) | async-done | bytes 8388640 | tf_op jit(solution)/shard_map/all_to_all | solution.py:97
  211.3 3.6 %all-to-all-start.1 = ((bf16[8,2,2,64,256]{4,3,2,1,0:T(8,128)(2,1)}), bf16[8,2,2,64,256]{4,3,2,1,0:T(8,128)(2,1)S(1)}, u32[]{:S(2)}, u32[]{:S(2)}) async-start(bf16[8,2,2,64,256]{4,3,2,1,0:T(8,128)(2,1)} %bitcast.7), calls=%async_computation.1 | async-start | bytes 2097152 | tf_op jit(solution)/shard_map/all_to_all | solution.py:98
  214.9 5.3 %fusion.29 = (f32[32,2,8]{2,1,0:T(2,128)}, f32[32,2,8,512]{3,2,1,0:T(8,128)S(1)}) fusion(bf16[32,2,8,128]{3,2,1,0:T(8,128)(2,1)S(1)} %bitcast.105, bf16[32,512,2,128]{1,3,2,0:T(8,128)(2,1)} %bitcast.99, pred[32,512]{1,0:T(8,128)(4,1)S(1)} %iota_compare_fusion), kind=kOutput, calls=%fused_computation.95 | convolution fusion | flops 67894784 | bytes 9586688 | tf_op jit(solution)/shard_map/bhgd,bthd->bhgt/dot_general | solution.py:126
  220.2 0.8 copy.95
  221.0 0.7 fusion.24
  221.7 0.8 iota_compare_fusion.2
  222.5 1.4 multiply_cosine_fusion
  223.8 5.2 %fusion.10 = f32[8,2,4,128]{3,2,1,0:T(4,128)} fusion(bf16[8,2,2048,128]{3,2,1,0:T(8,128)(2,1)} %all-to-all-done.2, bf16[8,2,4,2048]{3,2,1,0:T(4,128)(2,1)S(1)} %reshape.408, pred[8,2,4]{2,1,0:T(4,128)(4,1)S(1)} %iota_compare_fusion.2), kind=kOutput, calls=%fused_computation.26 | convolution fusion | flops 33685504 | bytes 8683584 | tf_op jit(solution)/shard_map/oksd,okdr->oksr/dot_general | solution.py:99
  229.1 12.1 %psum.7 = bf16[8,2,4,128]{3,2,1,0:T(4,128)(2,1)S(1)} all-reduce(f32[8,2,4,128]{3,2,1,0:T(4,128)} %fusion.10), channel_id=1, replica_groups=mesh['replica'=8,'tensor'=4] {'tensor'}, use_global_device_ids=true, to_apply=%region_6.7 | all-reduce | flops 8192 | bytes 49152 | tf_op jit(solution)/shard_map/psum | solution.py:102
  241.6 0.6 gather_fusion.7
  242.2 6.2 %convolution_add_fusion.1 = f32[32,2,256]{2,0,1:T(8,128)S(1)} fusion(bf16[2,256,8192]{2,1,0:T(8,128)(2,1)} %bitcast.101, bf16[32,8192]{1,0:T(8,128)(2,1)} %copy-done.2, f32[32,2,256]{2,1,0:T(2,128)S(1)} %gather_fusion.7), kind=kOutput, calls=%fused_computation.16 | convolution fusion | flops 268451840 | bytes 9043968 | tf_op jit(solution)/shard_map/dot_general | solution.py:110
  248.8 0.6 copy.102
  250.5 5.7 %fusion.1 = bf16[32,2,8,128]{3,2,1,0:T(8,128)(2,1)S(1)} fusion(bf16[32,512,2,128]{1,3,2,0:T(8,128)(2,1)} %bitcast.103, f32[32,2,8,512]{3,2,1,0:T(8,128)S(1)} %get-tuple-element.27, f32[32,2,8]{2,1,0:T(2,128)S(1)} %copy.98, f32[32,2,8]{2,1,0:T(2,128)S(1)} %copy.96, f32[32,2,128]{2,1,0:T(2,128)S(1)} %reshape.382, f32[32,2,8]{2,1,0:T(2,128)S(1)} %copy.101), kind=kOutput, calls=%fused_computation.13 | convolution fusion | flops 68091904 | bytes 9607168 | tf_op jit(solution)/shard_map/bhgt,bthd->bhgd/dot_general | solution.py:143
  256.2 0.7 copy.118
  (82 shorter events, 4.9 us)
Async XLA Ops:
  0.6 167.3 %copy-start = (bf16[16,2,64,256]{3,2,1,0:T(8,128)(2,1)S(1)}, bf16[16,2,64,256]{3,2,1,0:T(8,128)(2,1)}, u32[]{:S(2)}) copy-start(bf16[16,2,64,256]{3,2,1,0:T(8,128)(2,1)} %param.14) | copy-start | bytes 3145732
  24.4 186.9 %all-to-all-start.2 = ((bf16[8,2,2048,128]{3,2,1,0:T(8,128)(2,1)}), bf16[8,2,2048,128]{3,2,1,0:T(8,128)(2,1)}, u32[]{:S(2)}, u32[]{:S(2)}) async-start(bf16[8,2,2048,128]{3,2,1,0:T(8,128)(2,1)} %bitcast.100), calls=%async_computation.2 | async-start | bytes 16777216 | tf_op jit(solution)/shard_map/all_to_all | solution.py:97
  37.4 11.4 %copy-start.1 = (s32[1,16]{1,0:T(1,128)S(1)}, s32[1,16]{1,0:T(1,128)}, u32[]{:S(2)}) copy-start(s32[1,16]{1,0:T(1,128)} %param.18) | copy-start | bytes 196
  48.7 2.5 copy-start.3
  48.7 9.9 %copy-start.8 = (f32[8192]{0:T(1024)S(1)}, f32[8192]{0:T(1024)}, u32[]{:S(2)}) copy-start(f32[8192]{0:T(1024)} %param.11) | copy-start | bytes 98308
  48.7 14.5 %copy-start.9 = (s32[32]{0:T(128)S(1)}, s32[32]{0:T(128)}, u32[]{:S(2)}) copy-start(s32[32]{0:T(128)} %param.19) | copy-start | bytes 388
  51.0 7.7 %copy-start.7 = (s32[8,2]{1,0:T(8,128)}, s32[8,2]{1,0:T(8,128)S(1)}, u32[]{:S(2)}) copy-start(s32[8,2]{1,0:T(8,128)S(1)} %copy.87) | copy-start | bytes 196
  58.9 0.8 copy-start.2
  96.7 35.5 %copy-start.4 = (bf16[32,2048]{1,0:T(8,128)(2,1)S(1)}, bf16[32,2048]{1,0:T(8,128)(2,1)}, u32[]{:S(2)}) copy-start(bf16[32,2048]{1,0:T(8,128)(2,1)} %param.15) | copy-start | bytes 393220
  211.3 30.0 %all-to-all-start.1 = ((bf16[8,2,2,64,256]{4,3,2,1,0:T(8,128)(2,1)}), bf16[8,2,2,64,256]{4,3,2,1,0:T(8,128)(2,1)S(1)}, u32[]{:S(2)}, u32[]{:S(2)}) async-start(bf16[8,2,2,64,256]{4,3,2,1,0:T(8,128)(2,1)} %bitcast.7), calls=%async_computation.1 | async-start | bytes 2097152 | tf_op jit(solution)/shard_map/all_to_all | solution.py:98
  229.1 19.4 %copy-start.5 = (f32[32,64]{1,0:T(8,128)S(1)}, f32[32,64]{1,0:T(8,128)}, u32[]{:S(2)}) copy-start(f32[32,64]{1,0:T(8,128)} %get-tuple-element.22) | copy-start | bytes 24580
  229.1 19.4 %copy-start.6 = (f32[32,64]{1,0:T(8,128)S(1)}, f32[32,64]{1,0:T(8,128)}, u32[]{:S(2)}) copy-start(f32[32,64]{1,0:T(8,128)} %get-tuple-element.23) | copy-start | bytes 24580
where the time goes:
time: 260 us; the launch traced here: 257 us
  local copies, waits for them, and re-layouts  143 us (55%)
  waiting for transfers between devices  41.7 us (16%)
  blocking collectives  32.8 us (13%)
  matrix products  22.9 us (9%)
  starting transfers between devices  8.57 us (3%)
  other arithmetic  6.85 us (3%)
    unnamed x26, local copies, waits for them, and re-layouts  81.3 us
    all_to_all x1, waiting for transfers between devices, body(): lax.all_to_all(selected_down, 'replica', split_axis=0, concat_axis=0, til...  41.7 us
    slice x1, local copies, waits for them, and re-layouts, body(): key_value_cache[:, :, 0].reshape(row_count, cache_len, kv_local, HEAD)  33 us
    all_to_all x1, blocking collectives, body(): lax.all_to_all(wanted, 'replica', split_axis=0, concat_axis=0, tiled=True)  13.5 us
    psum x1, blocking collectives, body(): summed = lax.psum(partial_value, 'tensor').astype(jnp.bfloat16)  12.1 us
    dot_general x1, local copies, waits for them, and re-layouts, body(): jnp.dot(normed, key_value_weight.reshape(key_value_weight.shape[0], 2 * k...  11.3 us
    gather x1, local copies, waits for them, and re-layouts, body(): selected_down = adapter_down[segment_member_mask]  8.13 us
    all_gather x1, blocking collectives, body(): gathered = lax.all_gather(hidden, 'tensor', axis=1, tiled=True)  7.2 us
  transfers between devices with their start and end apart: 2, of which 1 were waited for; matrix products, arithmetic and copies ran while one was open for 57% of the time, Pallas kernels for 0%

commit v1 on v0

--- a/solution.py
+++ b/solution.py
@@ -10,6 +10,11 @@
 ADAPTER_SCALE = 0.5
 ROPE_BASE = 500000.0
 EPSILON = 1e-05
+
+
+def arrays_wrap(v0):
+    seen_now = jnp.sum(lax.all_gather(v0, "tensor"), axis=0)
+    return seen_now
 
 
 def rotate(key_heads, token_position):
@@ -99,7 +104,7 @@
     partial_value = jnp.einsum(
         "oksd,okdr->oksr", slot_rows, down_got, preferred_element_type=jnp.float32
     )
-    summed = lax.psum(partial_value, "tensor").astype(jnp.bfloat16)
+    summed = arrays_wrap(partial_value).astype(jnp.bfloat16)
     summed = summed.reshape(summed.shape[:3] + (2, adapter_rank_size))
     slot_delta = (
         jnp.einsum("okscr,okcrw->okscw", summed, up_got, preferred_element_type=jnp.float32)

time: 260 us -> 259 us (level)
  waiting for transfers between devices: 41.7 us -> 48.1 us
  blocking collectives: 32.8 us -> 26.5 us
    psum x1 -> x0, blocking collectives: 12.1 us -> none  [body(): summed = lax.psum(partial_value, 'tensor').astype(jnp.bfloat16)]
    all_to_all x1, waiting for transfers between devices: 0.01 us -> 6.45 us  [body(): lax.all_to_all(selected_up, 'replica', split_axis=0, concat_axis=0, tiled...]
    all_gather x0 -> x1, blocking collectives: none -> 5.74 us  [arrays_wrap(): seen_now = jnp.sum(lax.all_gather(v0, 'tensor'), axis=0)]
  transfers between devices with their start and end apart: 2 -> 2, of which waited for: 1 -> 2; matrix products, arithmetic and copies ran while one was open for 57% -> 57% of each run, Pallas kernels for 0% -> 0%
where the time goes in v1:
time: 259 us; the launch traced here: 257 us
  local copies, waits for them, and re-layouts  143 us (55%)
  waiting for transfers between devices  48.1 us (19%)
  blocking collectives  26.5 us (10%)
  matrix products  22.2 us (9%)
  starting transfers between devices  8.57 us (3%)
  other arithmetic  6.99 us (3%)
    unnamed x26, local copies, waits for them, and re-layouts  81.3 us
    all_to_all x1, waiting for transfers between devices, body(): lax.all_to_all(selected_down, 'replica', split_axis=0, concat_axis=0, til...  41.7 us
    slice x1, local copies, waits for them, and re-layouts, body(): key_value_cache[:, :, 0].reshape(row_count, cache_len, kv_local, HEAD)  33 us
    all_to_all x1, blocking collectives, body(): lax.all_to_all(wanted, 'replica', split_axis=0, concat_axis=0, tiled=True)  13.5 us
    dot_general x1, local copies, waits for them, and re-layouts, body(): jnp.dot(normed, key_value_weight.reshape(key_value_weight.shape[0], 2 * k...  11.3 us
    gather x1, local copies, waits for them, and re-layouts, body(): selected_down = adapter_down[segment_member_mask]  8.13 us
    all_gather x1, blocking collectives, body(): gathered = lax.all_gather(hidden, 'tensor', axis=1, tiled=True)  7.2 us
    all_to_all x1, waiting for transfers between devices, body(): lax.all_to_all(selected_up, 'replica', split_axis=0, concat_axis=0, tiled...  6.45 us
  transfers between devices with their start and end apart: 2, of which 2 were waited for; matrix products, arithmetic and copies ran while one was open for 57% of the time, Pallas kernels for 0%

profile of v1, /device:TPU:0, one launch (start us, length us, event | category | flops | bytes accessed | tf_op | source)
XLA Modules:
  0.0 256.5 jit_solution(3242119431928728630)
XLA Ops:
  0.6 0.8 fusion.26
  1.4 0.7 and_select_fusion.2
  2.5 13.5 %all_to_all.22 = s32[8,1,2]{2,1,0:T(1,128)S(1)} all-to-all(s32[8,1,2]{2,1,0:T(1,128)S(1)} %copy.84), channel_id=1, replica_groups=mesh['replica'=8,'tensor'=4] {'replica'}, dimensions={0} | all-to-all | bytes 128 | tf_op jit(solution)/shard_map/all_to_all | solution.py:99
  16.3 8.1 %gather_fusion.4 = bf16[16,2048,128]{2,1,0:T(8,128)(2,1)} fusion(bf16[16,2048,128]{2,1,0:T(8,128)(2,1)} %param.13, s32[1024]{0:T(1024)S(1)} %pad_clamp_fusion.4), kind=kCustom, calls=%fused_computation.4 | custom fusion | bytes 16777280 | tf_op jit(solution)/shard_map/gather | solution.py:100
  24.4 5.0 %all-to-all-start.2 = ((bf16[8,2,2048,128]{3,2,1,0:T(8,128)(2,1)}), bf16[8,2,2048,128]{3,2,1,0:T(8,128)(2,1)}, u32[]{:S(2)}, u32[]{:S(2)}) async-start(bf16[8,2,2048,128]{3,2,1,0:T(8,128)(2,1)} %bitcast.101), calls=%async_computation.2 | async-start | bytes 16777216 | tf_op jit(solution)/shard_map/all_to_all | solution.py:102
  29.4 8.0 %copy.114 = bf16[1024,8,2,256]{3,1,2,0:T(8,128)(2,1)} copy(bf16[1024,8,2,256]{3,2,1,0:T(2,128)(2,1)} %bitcast.105) | data formatting | bytes 16777216
  37.4 11.3 %copy.83 = bf16[512,8192]{1,0:T(8,128)(2,1)} copy(bf16[512,8192]{0,1:T(8,128)(2,1)} %bitcast.103) | data formatting | bytes 16777216 | tf_op jit(solution)/shard_map/dot_general | solution.py:115
  49.2 0.7 gather_fusion.2
  49.9 0.7 gather_fusion.1
  51.2 7.2 %all_gather.9 = bf16[32,8192]{1,0:T(8,128)(2,1)S(1)} all-gather(bf16[32,2048]{1,0:T(8,128)(2,1)S(1)} %copy-done.3), channel_id=1, replica_groups=mesh['replica'=8,'tensor'=4] {'tensor'}, dimensions={1}, use_global_device_ids=true | all-gather | bytes 655360 | tf_op jit(solution)/shard_map/all_gather | solution.py:59
  58.9 0.8 copy-done.2
  59.7 0.7 gather_fusion.3
  60.6 1.2 gather_fusion.6
  61.9 1.3 gather_fusion.5
  63.7 33.0 %fusion.28 = (bf16[32,512,1,256]{3,2,1,0:T(2,128)(2,1)}, bf16[32,512,1,256]{3,2,1,0:T(2,128)(2,1)}) fusion(bf16[32,512,2,256]{3,2,1,0:T(2,128)(2,1)} %param.16), kind=kLoop, calls=%fused_computation.94 | loop fusion | bytes 33554432 | tf_op jit(solution)/shard_map/slice | solution.py:128
  96.7 35.5 %copy.113 = bf16[32,512,1,256]{1,3,0,2:T(8,128)(2,1)} copy(bf16[32,512,1,256]{3,2,1,0:T(2,128)(2,1)} %get-tuple-element.17) | data formatting | bytes 16777216
  132.2 35.6 %copy.112 = bf16[32,512,1,256]{1,3,0,2:T(8,128)(2,1)} copy(bf16[32,512,1,256]{3,2,1,0:T(2,128)(2,1)} %get-tuple-element.16) | data formatting | bytes 16777216
  167.9 1.7 gather_fusion
  169.6 41.7 %all-to-all-done.2 = bf16[8,2,2048,128]{3,2,1,0:T(8,128)(2,1)} async-done(((bf16[8,2,2048,128]{3,2,1,0:T(8,128)(2,1)}), bf16[8,2,2048,128]{3,2,1,0:T(8,128)(2,1)}, u32[]{:S(2)}, u32[]{:S(2)}) %all-to-all-start.2) | async-done | bytes 8388640 | tf_op jit(solution)/shard_map/all_to_all | solution.py:102
  211.3 3.6 %all-to-all-start.1 = ((bf16[8,2,2,64,256]{4,3,2,1,0:T(8,128)(2,1)}), bf16[8,2,2,64,256]{4,3,2,1,0:T(8,128)(2,1)S(1)}, u32[]{:S(2)}, u32[]{:S(2)}) async-start(bf16[8,2,2,64,256]{4,3,2,1,0:T(8,128)(2,1)} %bitcast.7), calls=%async_computation.1 | async-start | bytes 2097152 | tf_op jit(solution)/shard_map/all_to_all | solution.py:103
  214.9 5.3 %fusion.29 = (f32[32,2,8]{2,1,0:T(2,128)}, f32[32,2,8,512]{3,2,1,0:T(8,128)S(1)}) fusion(bf16[32,2,8,128]{3,2,1,0:T(8,128)(2,1)S(1)} %bitcast.106, bf16[32,512,2,128]{1,3,2,0:T(8,128)(2,1)} %bitcast.100, pred[32,512]{1,0:T(8,128)(4,1)S(1)} %iota_compare_fusion), kind=kOutput, calls=%fused_computation.95 | convolution fusion | flops 67894784 | bytes 9586688 | tf_op jit(solution)/shard_map/bhgd,bthd->bhgt/dot_general | solution.py:131
  220.2 0.8 copy.98
  221.0 0.7 fusion.24
  221.7 0.8 iota_compare_fusion.2
  222.5 1.4 multiply_cosine_fusion
  223.9 4.6 %fusion.10 = f32[8,2,4,128]{3,2,1,0:T(4,128)S(1)} fusion(bf16[8,2,2048,128]{3,2,1,0:T(8,128)(2,1)} %all-to-all-done.2, bf16[8,2,4,2048]{3,2,1,0:T(4,128)(2,1)S(1)} %reshape.407, pred[8,2,4]{2,1,0:T(4,128)(4,1)S(1)} %iota_compare_fusion.2), kind=kOutput, calls=%fused_computation.26 | convolution fusion | flops 33685504 | bytes 8683584 | tf_op jit(solution)/shard_map/oksd,okdr->oksr/dot_general | solution.py:104
  228.5 5.7 %all-gather = f32[32,2,4,128]{3,2,1,0:T(4,128)S(1)} all-gather(f32[8,2,4,128]{3,2,1,0:T(4,128)S(1)} %fusion.10), channel_id=2, replica_groups=mesh['replica'=8,'tensor'=4] {'tensor'}, dimensions={0}, use_global_device_ids=true | all-gather | bytes 163840 | tf_op jit(solution)/shard_map/all_gather | solution.py:16
  234.4 6.4 %all-to-all-done.1 = bf16[8,2,2,64,256]{4,3,2,1,0:T(8,128)(2,1)S(1)} async-done(((bf16[8,2,2,64,256]{4,3,2,1,0:T(8,128)(2,1)}), bf16[8,2,2,64,256]{4,3,2,1,0:T(8,128)(2,1)S(1)}, u32[]{:S(2)}, u32[]{:S(2)}) %all-to-all-start.1) | async-done | bytes 1048608 | tf_op jit(solution)/shard_map/all_to_all | solution.py:103
  241.8 6.2 %convolution_add_fusion.1 = f32[32,2,256]{2,0,1:T(8,128)S(1)} fusion(bf16[2,256,8192]{2,1,0:T(8,128)(2,1)} %bitcast.102, bf16[32,8192]{1,0:T(8,128)(2,1)} %copy-done.2, f32[32,2,256]{2,1,0:T(2,128)S(1)} %gather_fusion.7), kind=kOutput, calls=%fused_computation.16 | convolution fusion | flops 268451840 | bytes 9043968 | tf_op jit(solution)/shard_map/dot_general | solution.py:115
  248.4 0.6 copy.105
  250.1 5.7 %fusion.1 = bf16[32,2,8,128]{3,2,1,0:T(8,128)(2,1)S(1)} fusion(bf16[32,512,2,128]{1,3,2,0:T(8,128)(2,1)} %bitcast.104, f32[32,2,8,512]{3,2,1,0:T(8,128)S(1)} %get-tuple-element.27, f32[32,2,8]{2,1,0:T(2,128)S(1)} %copy.101, f32[32,2,8]{2,1,0:T(2,128)S(1)} %copy.99, f32[32,2,128]{2,1,0:T(2,128)S(1)} %reshape.381, f32[32,2,8]{2,1,0:T(2,128)S(1)} %copy.104), kind=kOutput, calls=%fused_computation.13 | convolution fusion | flops 68091904 | bytes 9607168 | tf_op jit(solution)/shard_map/bhgt,bthd->bhgd/dot_general | solution.py:148
  255.8 0.7 copy.123
  (83 shorter events, 5.6 us)
Async XLA Ops:
  0.6 167.3 %copy-start = (bf16[16,2,64,256]{3,2,1,0:T(8,128)(2,1)S(1)}, bf16[16,2,64,256]{3,2,1,0:T(8,128)(2,1)}, u32[]{:S(2)}) copy-start(bf16[16,2,64,256]{3,2,1,0:T(8,128)(2,1)} %param.14) | copy-start | bytes 3145732
  24.4 186.9 %all-to-all-start.2 = ((bf16[8,2,2048,128]{3,2,1,0:T(8,128)(2,1)}), bf16[8,2,2048,128]{3,2,1,0:T(8,128)(2,1)}, u32[]{:S(2)}, u32[]{:S(2)}) async-start(bf16[8,2,2048,128]{3,2,1,0:T(8,128)(2,1)} %bitcast.101), calls=%async_computation.2 | async-start | bytes 16777216 | tf_op jit(solution)/shard_map/all_to_all | solution.py:102
  37.4 11.4 %copy-start.1 = (s32[1,16]{1,0:T(1,128)S(1)}, s32[1,16]{1,0:T(1,128)}, u32[]{:S(2)}) copy-start(s32[1,16]{1,0:T(1,128)} %param.18) | copy-start | bytes 196
  48.7 2.5 copy-start.3
  48.7 9.9 %copy-start.8 = (f32[8192]{0:T(1024)S(1)}, f32[8192]{0:T(1024)}, u32[]{:S(2)}) copy-start(f32[8192]{0:T(1024)} %param.11) | copy-start | bytes 98308
  48.7 14.4 %copy-start.9 = (s32[32]{0:T(128)S(1)}, s32[32]{0:T(128)}, u32[]{:S(2)}) copy-start(s32[32]{0:T(128)} %param.19) | copy-start | bytes 388
  51.0 7.7 %copy-start.7 = (s32[8,2]{1,0:T(8,128)}, s32[8,2]{1,0:T(8,128)S(1)}, u32[]{:S(2)}) copy-start(s32[8,2]{1,0:T(8,128)S(1)} %copy.89) | copy-start | bytes 196
  58.9 0.8 copy-start.2
  96.7 35.5 %copy-start.4 = (bf16[32,2048]{1,0:T(8,128)(2,1)S(1)}, bf16[32,2048]{1,0:T(8,128)(2,1)}, u32[]{:S(2)}) copy-start(bf16[32,2048]{1,0:T(8,128)(2,1)} %param.15) | copy-start | bytes 393220
  211.3 29.6 %all-to-all-start.1 = ((bf16[8,2,2,64,256]{4,3,2,1,0:T(8,128)(2,1)}), bf16[8,2,2,64,256]{4,3,2,1,0:T(8,128)(2,1)S(1)}, u32[]{:S(2)}, u32[]{:S(2)}) async-start(bf16[8,2,2,64,256]{4,3,2,1,0:T(8,128)(2,1)} %bitcast.7), calls=%async_computation.1 | async-start | bytes 2097152 | tf_op jit(solution)/shard_map/all_to_all | solution.py:103
  228.5 19.5 %copy-start.5 = (f32[32,64]{1,0:T(8,128)S(1)}, f32[32,64]{1,0:T(8,128)}, u32[]{:S(2)}) copy-start(f32[32,64]{1,0:T(8,128)} %get-tuple-element.22) | copy-start | bytes 24580
  228.5 19.5 %copy-start.6 = (f32[32,64]{1,0:T(8,128)S(1)}, f32[32,64]{1,0:T(8,128)}, u32[]{:S(2)}) copy-start(f32[32,64]{1,0:T(8,128)} %get-tuple-element.23) | copy-start | bytes 24580
